TPU v7x, 32 devices: a whole 2x2x4 slice. The times are simulated.
32 devices in a mesh: shots: 2 (over y), gx: 4 (over z), gy: 4 (over x, core).
Axes of the slice: x: 2, y: 2, z: 4, core: 2. Of those that a mesh axis runs over, the one named last changes fastest.
Arguments:
- p_now: float32 [64, 64, 128], P(('shots', 'gx'), 'gy'), parts along dimension 0, may hold values from -6 to 6
- q_now: float32 [64, 64, 128], P(('shots', 'gx'), 'gy'), parts along dimension 0, may hold values from -6 to 6
- p_prev: float32 [64, 64, 128], P(('shots', 'gx'), 'gy'), parts along dimension 0, may hold values from -6 to 6
- q_prev: float32 [64, 64, 128], P(('shots', 'gx'), 'gy'), parts along dimension 0, may hold values from -6 to 6
- speed: float32 [32, 64, 128], P('gx', 'gy'), may hold values from 0.05 to 0.2
- epsilon: float32 [32, 64, 128], P('gx', 'gy'), may hold values from 0.05 to 0.35
- delta: float32 [32, 64, 128], P('gx', 'gy'), may hold values from 0 to 0.3
- theta: float32 [32, 64, 128], P('gx', 'gy'), may hold values from -1 to 1
- phi: float32 [32, 64, 128], P('gx', 'gy'), may hold values from -3.140625 to 3.140625
- snapshots: bfloat16 [2, 64, 64, 128], P(None, ('shots', 'gx'), 'gy'), parts along dimension 1, may hold values from -6 to 6
- traces: float32 [1024, 4096], P(None, ('shots', 'gx', 'gy')), parts along dimension 1, may hold values from -6 to 6
- time_steps: int32 [4], P('shots'), parts along dimension 0, may hold values from 0 to 1023
- rec_owner: int32 [4096, 1], P(('shots', 'gx', 'gy')), parts along dimension 0, may hold values from 0 to 3; in each aligned block of 128 rows (0 to 127, 128 to 255, ...) at most 64 rows name the same one
- rec_local: int32 [4096], P(('shots', 'gx', 'gy')), parts along dimension 0, may hold values from 0 to 16383
Outputs:
- p_next: float32 [64, 64, 128], P(('shots', 'gx'), 'gy'), parts along dimension 0
- q_next: float32 [64, 64, 128], P(('shots', 'gx'), 'gy'), parts along dimension 0
- p_mid: float32 [64, 64, 128], P(('shots', 'gx'), 'gy'), parts along dimension 0
- q_mid: float32 [64, 64, 128], P(('shots', 'gx'), 'gy'), parts along dimension 0
- image: float32 [64, 64, 128], P(('shots', 'gx'), 'gy'), parts along dimension 0
There are 2 independent parts, one for each index of `shots`. A program takes and returns all parts, laid end to end along the dimension named above; an argument that names none is the same for every part. Nothing has to cross between parts.
Inputs may be any that keep to these rules, and one draw needn't show every extreme that they name: `rec_owner`: the 128 receivers of one device (aligned blocks of 128 rows) name any one owner at most 64 times, a bound that some block reaches. `rec_local`: A receiver's cell lies in the band of the second dimension that the device holding the receiver covers.
All inputs are finite; a program needn't handle non-finite values.
Results may differ from a plain program's by a relative error of at most 0.0003.
Values sent between devices are 32-bit elements; how exact they have to be, the bound alone decides.
No kernel may reach another device: no remote copies, remote signals or barrier semaphores. Data moves between devices by JAX's collectives and lax.ppermute only.
A program may use at most 64 MiB of HBM per device.

v0:
```python
import jax
import jax.numpy as jnp
from jax import lax
from jax.sharding import PartitionSpec as P

second_coef = (-205.0 / 72.0, 8.0 / 5.0, -1.0 / 5.0, 8.0 / 315.0, -1.0 / 560.0)
first_coef = (4.0 / 5.0, -1.0 / 5.0, 4.0 / 105.0, -1.0 / 280.0)


def padded_2(cells, sides, width):
    for axis, dim in sides:
        count = lax.axis_size(axis)
        ends = count - 1
        head = lax.slice_in_dim(cells, 0, width, axis=dim)
        tail = lax.slice_in_dim(cells, cells.shape[dim] - width, cells.shape[dim], axis=dim)
        cells = jnp.concatenate(
            [
                lax.ppermute(tail, axis, [(i, (i + 1) % count) for i in range(ends)]),
                cells,
                lax.ppermute(head, axis, [((i + 1) % count, i) for i in range(ends)]),
            ],
            axis=dim,
        )
    return cells


def derivatives(padded, sx, sy, sz):

    def part(dx, dy, dz):
        return padded[:, 4 + dx : 4 + dx + sx, 4 + dy : 4 + dy + sy, 4 + dz : 4 + dz + sz]

    centre = part(0, 0, 0)
    dxx = second_coef[0] * centre
    dyy = second_coef[0] * centre
    dzz = second_coef[0] * centre
    for k in range(1, 5):
        dxx = dxx + second_coef[k] * (part(k, 0, 0) + part(-k, 0, 0))
        dyy = dyy + second_coef[k] * (part(0, k, 0) + part(0, -k, 0))
        dzz = dzz + second_coef[k] * (part(0, 0, k) + part(0, 0, -k))
    dy_wide = 0.0
    dz_xwide = 0.0
    dz_ywide = 0.0
    for k in range(1, 5):
        weight = first_coef[k - 1]
        dy_wide = dy_wide + weight * (
            padded[:, :, 4 + k : 4 + k + sy, 4 : 4 + sz]
            - padded[:, :, 4 - k : 4 - k + sy, 4 : 4 + sz]
        )
        dz_xwide = dz_xwide + weight * (
            padded[:, :, 4 : 4 + sy, 4 + k : 4 + k + sz]
            - padded[:, :, 4 : 4 + sy, 4 - k : 4 - k + sz]
        )
        dz_ywide = dz_ywide + weight * (
            padded[:, 4 : 4 + sx, :, 4 + k : 4 + k + sz]
            - padded[:, 4 : 4 + sx, :, 4 - k : 4 - k + sz]
        )
    dxy = 0.0
    dxz = 0.0
    dyz = 0.0
    for k in range(1, 5):
        weight = first_coef[k - 1]
        dxy = dxy + weight * (dy_wide[:, 4 + k : 4 + k + sx] - dy_wide[:, 4 - k : 4 - k + sx])
        dxz = dxz + weight * (dz_xwide[:, 4 + k : 4 + k + sx] - dz_xwide[:, 4 - k : 4 - k + sx])
        dyz = dyz + weight * (
            dz_ywide[:, :, 4 + k : 4 + k + sy] - dz_ywide[:, :, 4 - k : 4 - k + sy]
        )
    return (centre, dxx, dyy, dzz, dxy, dxz, dyz)


def advance(padded, previous, speed, epsilon, delta, theta, phi, source):
    sx, sy, sz = (previous.shape[1], previous.shape[2], previous.shape[3])
    centre, dxx, dyy, dzz, dxy, dxz, dyz = derivatives(padded, sx, sy, sz)
    axis_x = jnp.sin(theta) * jnp.cos(phi)
    axis_y = jnp.sin(theta) * jnp.sin(phi)
    axis_z = jnp.cos(theta)
    rotated = (
        axis_x * axis_x * dxx
        + axis_y * axis_y * dyy
        + axis_z * axis_z * dzz
        + 2.0 * axis_x * axis_y * dxy
        + 2.0 * axis_x * axis_z * dxz
        + 2.0 * axis_y * axis_z * dyz
    )
    remainder = dxx + dyy + dzz - rotated
    root_delta = jnp.sqrt(1.0 + 2.0 * delta)
    p_new = (
        2.0 * centre[0]
        - previous[0]
        + speed * ((1.0 + 2.0 * epsilon) * remainder[0] + root_delta * rotated[1])
        + source
    )
    q_new = (
        2.0 * centre[1] - previous[1] + speed * (root_delta * remainder[0] + rotated[1]) + source
    )
    return jnp.stack([p_new, q_new])


def pad_depth(fields):
    return jnp.pad(fields, ((0, 0), (0, 0), (0, 0), (4, 4)))


def widened(fields):
    return pad_depth(padded_2(fields, (("gx", 1), ("gy", 2)), 4))


def local(
    p_now,
    q_now,
    p_prev,
    q_prev,
    speed,
    epsilon,
    delta,
    theta,
    phi,
    snapshots,
    traces,
    time_steps,
    rec_owner,
    rec_local,
):
    sx, sy, sz = p_now.shape
    cells = sx * sy * sz
    groups = lax.axis_size("gx")
    held = rec_local.shape[0]
    samples = jnp.take(traces, time_steps, axis=0)
    owner = rec_owner[:, 0]
    capacity = 2 * held // groups
    onehot = (owner[:, None] == jnp.arange(groups, dtype=jnp.int32)[None, :]).astype(jnp.int32)
    running = jnp.cumsum(onehot, axis=0)
    rank = jnp.sum(onehot * running, axis=1) - 1
    position = owner * capacity + rank
    payload = jnp.concatenate([samples, rec_local.astype(jnp.float32)[None, :]], axis=0)
    slots = jnp.zeros((3, groups * capacity), jnp.float32).at[:, position].set(payload)
    slots = slots.reshape(3, groups, capacity)
    arrived = lax.all_to_all(slots, "gx", split_axis=1, concat_axis=1, tiled=True)
    values = arrived[0:2].reshape(2, groups * capacity)
    target = arrived[2].reshape(groups * capacity).astype(jnp.int32)
    sources = jnp.zeros((2, cells), jnp.float32).at[:, target].add(values).reshape(2, sx, sy, sz)
    current = jnp.stack([p_now, q_now])
    earlier = jnp.stack([p_prev, q_prev])
    middle = advance(widened(current), earlier, speed, epsilon, delta, theta, phi, sources[0])
    final = advance(widened(middle), current, speed, epsilon, delta, theta, phi, sources[1])
    image = (
        snapshots[0].astype(jnp.float32) * middle[0] + snapshots[1].astype(jnp.float32) * final[0]
    )
    return (final[0], final[1], middle[0], middle[1], image)


def solution(mesh):
    return jax.shard_map(
        local,
        mesh=mesh,
        in_specs=(
            P(("shots", "gx"), "gy", None),
            P(("shots", "gx"), "gy", None),
            P(("shots", "gx"), "gy", None),
            P(("shots", "gx"), "gy", None),
            P("gx", "gy", None),
            P("gx", "gy", None),
            P("gx", "gy", None),
            P("gx", "gy", None),
            P("gx", "gy", None),
            P(None, ("shots", "gx"), "gy", None),
            P(None, ("shots", "gx", "gy")),
            P("shots"),
            P(("shots", "gx", "gy"), None),
            P(("shots", "gx", "gy")),
        ),
        out_specs=(
            P(("shots", "gx"), "gy", None),
            P(("shots", "gx"), "gy", None),
            P(("shots", "gx"), "gy", None),
            P(("shots", "gx"), "gy", None),
            P(("shots", "gx"), "gy", None),
        ),
        check_vma=False,
    )
```

profile of v0, /device:TPU:18, one launch (start us, length us, event | category | flops | bytes accessed | tf_op | source)
XLA Modules:
  0.0 71.5 jit_solution(5272176775762559091)
XLA Ops:
  0.6 0.7 %compare_select_fusion.1 = s32[2]{0:T(128)S(1)} fusion(s32[2]{0:T(128)} %param.25), kind=kLoop, calls=%fused_computation.299 | loop fusion | flops 6 | bytes 16 | tf_op jit(solution)/shard_map/jit(_take)/jit(_where)/select_n | solution.py:126
  1.4 0.7 compare_and_fusion
  2.0 0.7 %fusion.156 = s32[128,4]{1,0:T(8,128)S(1)} fusion(s32[128]{0:T(128)} %bitcast.80), kind=kLoop, calls=%fused_computation.286 | loop fusion | flops 1024 | bytes 2560 | tf_op jit(solution)/shard_map/convert_element_type | solution.py:129
  2.8 0.2 reduce_window_sum.11
  2.9 0.8 %select_reduce_fusion = s32[128]{0:T(128)S(1)} fusion(s32[128,4]{1,0:T(8,128)S(1)} %reduce_window_sum.11, s32[128]{0:T(128)} %bitcast.81), kind=kLoop, calls=%fused_computation.284 | loop fusion | flops 1408 | bytes 3072 | tf_op jit(solution)/shard_map/reduce_sum | solution.py:131
  3.8 0.7 fusion.160
  4.4 0.7 convert_bitcast_fusion
  5.1 0.6 gather_fusion
  5.7 0.1 broadcast_select_fusion
  5.8 0.1 copy.25
  5.9 0.9 %scatter_custom_fusion = f32[3,256]{0,1:T(8,128)S(1)} fusion(s32[128]{0:T(128)S(1)} %fusion.160, f32[128,3]{1,0:T(8,128)S(1)} %copy.25, f32[]{:T(128)} %constant.26.clone.1), kind=kCustom, calls=%fused_computation.287 | custom fusion | bytes 3076 | tf_op jit(solution)/shard_map/scatter | solution.py:134
  6.8 0.1 copy.26
  6.9 0.7 reshape.111
  7.6 5.2 %all-to-all-start = ((f32[4,1,192]{2,1,0:T(1,128)}), f32[4,1,192]{2,1,0:T(1,128)S(1)}, u32[]{:S(2)}, u32[]{:S(2)}) async-start(f32[4,1,192]{2,1,0:T(1,128)} %reshape.111), calls=%async_computation | async-start | bytes 8192 | tf_op jit(solution)/shard_map/all_to_all | solution.py:136
  12.8 0.8 %fusion.152 = (f32[2,4,16,128]{3,2,1,0:T(8,128)S(1)}, f32[2,4,16,128]{3,2,1,0:T(8,128)S(1)}) fusion(f32[1,8,16,128]{3,2,1,0:T(8,128)} %bitcast.59, f32[1,8,16,128]{3,2,1,0:T(8,128)} %bitcast.47), kind=kLoop, calls=%fused_computation.259 | loop fusion | flops 32768 | bytes 262144 | tf_op jit(solution)/shard_map/stack | solution.py:140
  13.6 2.5 %collective-permute-start = (f32[2,4,16,128]{3,2,1,0:T(8,128)S(1)}, f32[2,4,16,128]{3,2,1,0:T(8,128)S(1)}, u32[]{:S(2)}, u32[]{:S(2)}) collective-permute-start(f32[2,4,16,128]{3,2,1,0:T(8,128)S(1)} %get-tuple-element.42), channel_id=1, source_target_pairs={{4,0},{8,4},{12,8},{5,1},{9,5},{13,9},{6,2},{10,6},{14,10},{7,3},{... | collective-permute-start | bytes 196616 | tf_op jit(solution)/shard_map/ppermute | solution.py:20
  16.1 3.4 %collective-permute-start.1 = (f32[2,4,16,128]{3,2,1,0:T(8,128)S(1)}, f32[2,4,16,128]{3,2,1,0:T(8,128)S(1)}, u32[]{:S(2)}, u32[]{:S(2)}) collective-permute-start(f32[2,4,16,128]{3,2,1,0:T(8,128)S(1)} %get-tuple-element.41), channel_id=1, source_target_pairs={{0,4},{4,8},{8,12},{1,5},{5,9},{9,13},{2,6},{6,10},{10,14},{3,7},{... | collective-permute-start | bytes 196616 | tf_op jit(solution)/shard_map/ppermute | solution.py:18
  19.4 1.1 %fusion.171 = (f32[8,16,128]{2,1,0:T(8,128)S(1)}, f32[8,16,128]{2,1,0:T(8,128)S(1)}) fusion(f32[8,16,128]{2,1,0:T(8,128)} %param.21), kind=kLoop, calls=%fused_computation.311 | loop fusion | bytes 196608 | tf_op jit(solution)/shard_map/sin | solution.py:73
  20.5 1.1 %fusion.161 = (f32[8,16,128]{2,1,0:T(8,128)S(1)}, f32[8,16,128]{2,1,0:T(8,128)S(1)}, f32[8,16,128]{2,1,0:T(8,128)S(1)}, f32[8,16,128]{2,1,0:T(8,128)S(1)}, f32[8...) fusion(f32[8,16,128]{2,1,0:T(8,128)S(1)} %get-tuple-element.44, f32[8,16,128]{2,1,0:T(8,128)} %param.22, ...), kind=kLoop, calls=%fused_computation.309 | loop fusion | flops 163840 | bytes 589824 | tf_op jit(solution)/shard_map/mul | solution.py:77
  21.6 0.5 broadcast.301
  22.2 0.7 reduce.8
  22.8 0.1 reshape.112
  22.9 0.1 convert_element_type.37
  23.0 0.1 reshape.90
  23.1 0.1 copy.28
  23.3 5.1 %scatter_custom_fusion.1 = f32[2,16384]{0,1:T(8,128)} fusion(s32[256]{0:T(256)S(1)} %bitcast.82, f32[256,2]{1,0:T(8,128)S(1)} %copy.28, f32[]{:T(128)} %constant.26.clone.1), kind=kCustom, calls=%fused_computation.5 | custom fusion | flops 512 | bytes 131076 | tf_op jit(solution)/shard_map/scatter-add | solution.py:139
  28.4 12.3 %slice_reduce_fusion.1 = (f32[16384]{0:T(1024)S(1)}, f32[16384]{0:T(1024)S(1)}) fusion(f32[2,16384]{0,1:T(8,128)} %scatter_custom_fusion.1), kind=kLoop, calls=%fused_computation.4 | loop fusion | bytes 262144 | tf_op jit(solution)/shard_map/slice | solution.py:142
  40.8 1.9 %collective-permute-start.2 = (f32[2,16,4,128]{3,2,1,0:T(4,128)S(1)}, f32[2,16,4,128]{3,2,1,0:T(4,128)S(1)}, u32[]{:S(2)}, u32[]{:S(2)}) collective-permute-start(f32[2,16,4,128]{3,2,1,0:T(4,128)S(1)} %get-tuple-element.27), channel_id=1, source_target_pairs={{1,0},{2,1},{3,2},{5,4},{6,5},{7,6},{9,8},{10,9},{11,10},{13,12},{... | collective-permute-start | bytes 196616 | tf_op jit(solution)/shard_map/ppermute | solution.py:20
  42.8 2.5 %collective-permute-start.3 = (f32[2,16,4,128]{3,2,1,0:T(4,128)S(1)}, f32[2,16,4,128]{3,2,1,0:T(4,128)S(1)}, u32[]{:S(2)}, u32[]{:S(2)}) collective-permute-start(f32[2,16,4,128]{3,2,1,0:T(4,128)S(1)} %get-tuple-element.26), channel_id=1, source_target_pairs={{0,1},{1,2},{2,3},{4,5},{5,6},{6,7},{8,9},{9,10},{10,11},{12,13},{... | collective-permute-start | bytes 196616 | tf_op jit(solution)/shard_map/ppermute | solution.py:18
  45.4 3.1 %collective-permute-done.3 = f32[2,16,4,128]{3,2,1,0:T(4,128)S(1)} collective-permute-done((f32[2,16,4,128]{3,2,1,0:T(4,128)S(1)}, f32[2,16,4,128]{3,2,1,0:T(4,128)S(1)}, u32[]{:S(2)}, u32[]{:S(2)}) %collective-permute-start.3) | collective-permute-done | bytes 65568 | tf_op jit(solution)/shard_map/ppermute | solution.py:18
  48.5 0.4 select_maximum_fusion.5
  48.9 0.4 fusion.39
  49.4 0.7 fusion.18
  50.1 0.6 fusion.101
  50.9 3.1 %collective-permute-start.4 = (f32[2,4,16,128]{3,2,1,0:T(8,128)S(1)}, f32[2,4,16,128]{3,2,1,0:T(8,128)S(1)}, u32[]{:S(2)}, u32[]{:S(2)}) collective-permute-start(f32[2,4,16,128]{3,2,1,0:T(8,128)S(1)} %get-tuple-element.33), channel_id=1, source_target_pairs={{4,0},{8,4},{12,8},{5,1},{9,5},{13,9},{6,2},{10,6},{14,10},{7,3},{... | collective-permute-start | bytes 196616 | tf_op jit(solution)/shard_map/ppermute | solution.py:20
  54.0 2.7 %collective-permute-start.5 = (f32[2,4,16,128]{3,2,1,0:T(8,128)S(1)}, f32[2,4,16,128]{3,2,1,0:T(8,128)S(1)}, u32[]{:S(2)}, u32[]{:S(2)}) collective-permute-start(f32[2,4,16,128]{3,2,1,0:T(8,128)S(1)} %get-tuple-element.32), channel_id=1, source_target_pairs={{0,4},{4,8},{8,12},{1,5},{5,9},{9,13},{2,6},{6,10},{10,14},{3,7},{... | collective-permute-start | bytes 196616 | tf_op jit(solution)/shard_map/ppermute | solution.py:18
  56.7 0.3 collective-permute-done.4
  57.0 3.1 %collective-permute-done.5 = f32[2,4,16,128]{3,2,1,0:T(8,128)S(1)} collective-permute-done((f32[2,4,16,128]{3,2,1,0:T(8,128)S(1)}, f32[2,4,16,128]{3,2,1,0:T(8,128)S(1)}, u32[]{:S(2)}, u32[]{:S(2)}) %collective-permute-start.5) | collective-permute-done | bytes 65568 | tf_op jit(solution)/shard_map/ppermute | solution.py:18
  60.2 1.9 %collective-permute-start.6 = (f32[2,16,4,128]{3,2,1,0:T(4,128)S(1)}, f32[2,16,4,128]{3,2,1,0:T(4,128)S(1)}, u32[]{:S(2)}, u32[]{:S(2)}) collective-permute-start(f32[2,16,4,128]{3,2,1,0:T(4,128)S(1)} %get-tuple-element.23), channel_id=1, source_target_pairs={{1,0},{2,1},{3,2},{5,4},{6,5},{7,6},{9,8},{10,9},{11,10},{13,12},{... | collective-permute-start | bytes 196616 | tf_op jit(solution)/shard_map/ppermute | solution.py:20
  62.1 2.5 %collective-permute-start.7 = (f32[2,16,4,128]{3,2,1,0:T(4,128)S(1)}, f32[2,16,4,128]{3,2,1,0:T(4,128)S(1)}, u32[]{:S(2)}, u32[]{:S(2)}) collective-permute-start(f32[2,16,4,128]{3,2,1,0:T(4,128)S(1)} %get-tuple-element.22), channel_id=1, source_target_pairs={{0,1},{1,2},{2,3},{4,5},{5,6},{6,7},{8,9},{9,10},{10,11},{12,13},{... | collective-permute-start | bytes 196616 | tf_op jit(solution)/shard_map/ppermute | solution.py:18
  64.7 3.1 %collective-permute-done.7 = f32[2,16,4,128]{3,2,1,0:T(4,128)S(1)} collective-permute-done((f32[2,16,4,128]{3,2,1,0:T(4,128)S(1)}, f32[2,16,4,128]{3,2,1,0:T(4,128)S(1)}, u32[]{:S(2)}, u32[]{:S(2)}) %collective-permute-start.7) | collective-permute-done | bytes 65568 | tf_op jit(solution)/shard_map/ppermute | solution.py:18
  67.8 0.4 select_maximum_fusion
  68.2 0.4 fusion.32
  68.7 0.5 fusion.4
  69.3 0.2 fusion.11
  69.5 0.6 fusion.50
  70.1 0.7 %fusion.155 = (f32[8,16,128]{2,1,0:T(8,128)}, f32[8,16,128]{2,1,0:T(8,128)}, f32[8,16,128]{2,1,0:T(8,128)S(1)}) fusion(f32[8,16,128]{2,1,0:T(8,128)S(1)} %add_add_fusion.3, bf16[2,8,16,128]{3,2,1,0:T(8,128)(2,1)S(1)} %copy-done.10, f32[8,16,128]{2,1,0:T(8,128)S(1)} %bitcast.73, f32[8,16,128]{2,1,0:T(8,128)S(1)} %copy-done.5, ...), kind=kLoop, calls=%fused_computation.279 | loop fusion | flops 327680 | bytes 983040 | tf_op jit(solution)/shard_map/add | solution.py:145
  70.8 0.7 add_add_fusion
  (42 shorter events, 0.5 us)
Async XLA Ops:
  0.6 4.5 %copy-start = (f32[1024,128]{1,0:T(8,128)S(1)}, f32[1024,128]{1,0:T(8,128)}, u32[]{:S(2)}) copy-start(f32[1024,128]{1,0:T(8,128)} %param.24) | copy-start | bytes 1572868
  7.6 14.1 %all-to-all-start = ((f32[4,1,192]{2,1,0:T(1,128)}), f32[4,1,192]{2,1,0:T(1,128)S(1)}, u32[]{:S(2)}, u32[]{:S(2)}) async-start(f32[4,1,192]{2,1,0:T(1,128)} %reshape.111), calls=%async_computation | async-start | bytes 8192 | tf_op jit(solution)/shard_map/all_to_all | solution.py:136
  13.6 27.1 %collective-permute-start = (f32[2,4,16,128]{3,2,1,0:T(8,128)S(1)}, f32[2,4,16,128]{3,2,1,0:T(8,128)S(1)}, u32[]{:S(2)}, u32[]{:S(2)}) collective-permute-start(f32[2,4,16,128]{3,2,1,0:T(8,128)S(1)} %get-tuple-element.42), channel_id=1, source_target_pairs={{4,0},{8,4},{12,8},{5,1},{9,5},{13,9},{6,2},{10,6},{14,10},{7,3},{... | collective-permute-start | bytes 196616 | tf_op jit(solution)/shard_map/ppermute | solution.py:20
  16.1 24.7 %collective-permute-start.1 = (f32[2,4,16,128]{3,2,1,0:T(8,128)S(1)}, f32[2,4,16,128]{3,2,1,0:T(8,128)S(1)}, u32[]{:S(2)}, u32[]{:S(2)}) collective-permute-start(f32[2,4,16,128]{3,2,1,0:T(8,128)S(1)} %get-tuple-element.41), channel_id=1, source_target_pairs={{0,4},{4,8},{8,12},{1,5},{5,9},{9,13},{2,6},{6,10},{10,14},{3,7},{... | collective-permute-start | bytes 196616 | tf_op jit(solution)/shard_map/ppermute | solution.py:18
  28.4 12.3 %copy-start.1 = (f32[8,16,128]{2,1,0:T(8,128)S(1)}, f32[8,16,128]{2,1,0:T(8,128)}, u32[]{:S(2)}) copy-start(f32[8,16,128]{2,1,0:T(8,128)} %param.15) | copy-start | bytes 196612
  28.4 12.3 %copy-start.3 = (f32[8,16,128]{2,1,0:T(8,128)S(1)}, f32[8,16,128]{2,1,0:T(8,128)}, u32[]{:S(2)}) copy-start(f32[8,16,128]{2,1,0:T(8,128)} %param.14) | copy-start | bytes 196612
  40.8 4.6 %collective-permute-start.2 = (f32[2,16,4,128]{3,2,1,0:T(4,128)S(1)}, f32[2,16,4,128]{3,2,1,0:T(4,128)S(1)}, u32[]{:S(2)}, u32[]{:S(2)}) collective-permute-start(f32[2,16,4,128]{3,2,1,0:T(4,128)S(1)} %get-tuple-element.27), channel_id=1, source_target_pairs={{1,0},{2,1},{3,2},{5,4},{6,5},{7,6},{9,8},{10,9},{11,10},{13,12},{... | collective-permute-start | bytes 196616 | tf_op jit(solution)/shard_map/ppermute | solution.py:20
  42.7 7.9 %copy-start.5 = (f32[8,16,128]{2,1,0:T(8,128)S(1)}, f32[8,16,128]{2,1,0:T(8,128)}, u32[]{:S(2)}) copy-start(f32[8,16,128]{2,1,0:T(8,128)} %param.18) | copy-start | bytes 196612
  42.7 7.9 %copy-start.6 = (f32[8,16,128]{2,1,0:T(8,128)S(1)}, f32[8,16,128]{2,1,0:T(8,128)}, u32[]{:S(2)}) copy-start(f32[8,16,128]{2,1,0:T(8,128)} %param.20) | copy-start | bytes 196612
  42.7 7.9 %copy-start.8 = (f32[8,16,128]{2,1,0:T(8,128)S(1)}, f32[8,16,128]{2,1,0:T(8,128)}, u32[]{:S(2)}) copy-start(f32[8,16,128]{2,1,0:T(8,128)} %param.17) | copy-start | bytes 196612
  42.8 5.7 %collective-permute-start.3 = (f32[2,16,4,128]{3,2,1,0:T(4,128)S(1)}, f32[2,16,4,128]{3,2,1,0:T(4,128)S(1)}, u32[]{:S(2)}, u32[]{:S(2)}) collective-permute-start(f32[2,16,4,128]{3,2,1,0:T(4,128)S(1)} %get-tuple-element.26), channel_id=1, source_target_pairs={{0,1},{1,2},{2,3},{4,5},{5,6},{6,7},{8,9},{9,10},{10,11},{12,13},{... | collective-permute-start | bytes 196616 | tf_op jit(solution)/shard_map/ppermute | solution.py:18
  45.3 5.4 %copy-start.7 = (f32[8,16,128]{2,1,0:T(8,128)S(1)}, f32[8,16,128]{2,1,0:T(8,128)}, u32[]{:S(2)}) copy-start(f32[8,16,128]{2,1,0:T(8,128)} %param.19) | copy-start | bytes 196612
  45.4 5.4 %copy-start.9 = (f32[8,16,128]{2,1,0:T(8,128)S(1)}, f32[8,16,128]{2,1,0:T(8,128)}, u32[]{:S(2)}) copy-start(f32[8,16,128]{2,1,0:T(8,128)} %param.16) | copy-start | bytes 196612
  50.7 20.1 %copy-start.2 = (f32[8,16,128]{2,1,0:T(8,128)}, f32[8,16,128]{2,1,0:T(8,128)S(1)}, u32[]{:S(2)}) copy-start(f32[8,16,128]{2,1,0:T(8,128)S(1)} %get-tuple-element.14) | copy-start | bytes 196612
  50.8 19.2 %copy-start.4 = (f32[8,16,128]{2,1,0:T(8,128)}, f32[8,16,128]{2,1,0:T(8,128)S(1)}, u32[]{:S(2)}) copy-start(f32[8,16,128]{2,1,0:T(8,128)S(1)} %add_add_fusion.3) | copy-start | bytes 196612
  50.9 6.2 %collective-permute-start.4 = (f32[2,4,16,128]{3,2,1,0:T(8,128)S(1)}, f32[2,4,16,128]{3,2,1,0:T(8,128)S(1)}, u32[]{:S(2)}, u32[]{:S(2)}) collective-permute-start(f32[2,4,16,128]{3,2,1,0:T(8,128)S(1)} %get-tuple-element.33), channel_id=1, source_target_pairs={{4,0},{8,4},{12,8},{5,1},{9,5},{13,9},{6,2},{10,6},{14,10},{7,3},{... | collective-permute-start | bytes 196616 | tf_op jit(solution)/shard_map/ppermute | solution.py:20
  54.0 6.2 %collective-permute-start.5 = (f32[2,4,16,128]{3,2,1,0:T(8,128)S(1)}, f32[2,4,16,128]{3,2,1,0:T(8,128)S(1)}, u32[]{:S(2)}, u32[]{:S(2)}) collective-permute-start(f32[2,4,16,128]{3,2,1,0:T(8,128)S(1)} %get-tuple-element.32), channel_id=1, source_target_pairs={{0,4},{4,8},{8,12},{1,5},{5,9},{9,13},{2,6},{6,10},{10,14},{3,7},{... | collective-permute-start | bytes 196616 | tf_op jit(solution)/shard_map/ppermute | solution.py:18
  60.2 4.5 %collective-permute-start.6 = (f32[2,16,4,128]{3,2,1,0:T(4,128)S(1)}, f32[2,16,4,128]{3,2,1,0:T(4,128)S(1)}, u32[]{:S(2)}, u32[]{:S(2)}) collective-permute-start(f32[2,16,4,128]{3,2,1,0:T(4,128)S(1)} %get-tuple-element.23), channel_id=1, source_target_pairs={{1,0},{2,1},{3,2},{5,4},{6,5},{7,6},{9,8},{10,9},{11,10},{13,12},{... | collective-permute-start | bytes 196616 | tf_op jit(solution)/shard_map/ppermute | solution.py:20
  62.1 8.0 %copy-start.10 = (bf16[2,8,16,128]{3,2,1,0:T(8,128)(2,1)S(1)}, bf16[2,8,16,128]{3,2,1,0:T(8,128)(2,1)}, u32[]{:S(2)}) copy-start(bf16[2,8,16,128]{3,2,1,0:T(8,128)(2,1)} %param.23) | copy-start | bytes 196612
  62.1 5.7 %collective-permute-start.7 = (f32[2,16,4,128]{3,2,1,0:T(4,128)S(1)}, f32[2,16,4,128]{3,2,1,0:T(4,128)S(1)}, u32[]{:S(2)}, u32[]{:S(2)}) collective-permute-start(f32[2,16,4,128]{3,2,1,0:T(4,128)S(1)} %get-tuple-element.22), channel_id=1, source_target_pairs={{0,1},{1,2},{2,3},{4,5},{5,6},{6,7},{8,9},{9,10},{10,11},{12,13},{... | collective-permute-start | bytes 196616 | tf_op jit(solution)/shard_map/ppermute | solution.py:18
where the time goes:
time: 72.1 us; the launch traced here: 71.5 us
  starting transfers between devices  25.8 us (36%)
  other arithmetic  18.3 us (25%)
  local copies, waits for them, and re-layouts  16.7 us (23%)
  waiting for transfers between devices  9.66 us (13%)
  between operations  1.04 us (1%)
    slice x1, local copies, waits for them, and re-layouts, local(): sources[0]  12.3 us
    ppermute x4, starting transfers between devices, padded_2(): lax.ppermute(tail, axis, [(i, (i + 1) % count) for i in range(ends)])  11.2 us
    ppermute x4, starting transfers between devices, padded_2(): lax.ppermute(head, axis, [((i + 1) % count, i) for i in range(ends)])  9.42 us
    ppermute x4, waiting for transfers between devices, padded_2(): lax.ppermute(tail, axis, [(i, (i + 1) % count) for i in range(ends)])  9.35 us
    all_to_all x1, starting transfers between devices, local(): lax.all_to_all(slots, 'gx', split_axis=1, concat_axis=1, tiled=True)  5.2 us
    scatter-add x1, other arithmetic, local(): jnp.zeros((2, cells), jnp.float32).at[:, target].add(values)  5.14 us
  transfers between devices with their start and end apart: 9, of which 4 were waited for; matrix products, arithmetic and copies ran while one was open for 31% of the time, Pallas kernels for 0%

commit v1 on v0

--- a/solution.py
+++ b/solution.py
@@ -133,7 +133,9 @@
     payload = jnp.concatenate([samples, rec_local.astype(jnp.float32)[None, :]], axis=0)
     slots = jnp.zeros((3, groups * capacity), jnp.float32).at[:, position].set(payload)
     slots = slots.reshape(3, groups, capacity)
-    arrived = lax.all_to_all(slots, "gx", split_axis=1, concat_axis=1, tiled=True)
+    arrived = jnp.concatenate(
+        lax.all_to_all(jnp.stack(jnp.split(slots, lax.axis_size("gx"), axis=1)), "gx", 0, 0), axis=1
+    )
     values = arrived[0:2].reshape(2, groups * capacity)
     target = arrived[2].reshape(groups * capacity).astype(jnp.int32)
     sources = jnp.zeros((2, cells), jnp.float32).at[:, target].add(values).reshape(2, sx, sy, sz)

time: 72.1 us -> 73.1 us (1.014)
  transfers between devices with their start and end apart: 9 -> 9, of which waited for: 4 -> 4; matrix products, arithmetic and copies ran while one was open for 31% -> 30% of each run, Pallas kernels for 0% -> 0%
where the time goes in v1:
time: 73.1 us; the launch traced here: 72.4 us
  starting transfers between devices  25.8 us (35%)
  other arithmetic  19 us (26%)
  local copies, waits for them, and re-layouts  16.9 us (23%)
  waiting for transfers between devices  9.66 us (13%)
  between operations  1.06 us (1%)
    slice x1, local copies, waits for them, and re-layouts, local(): sources[0]  12.3 us
    ppermute x4, starting transfers between devices, padded_2(): lax.ppermute(tail, axis, [(i, (i + 1) % count) for i in range(ends)])  11.2 us
    ppermute x4, starting transfers between devices, padded_2(): lax.ppermute(head, axis, [((i + 1) % count, i) for i in range(ends)])  9.42 us
    ppermute x4, waiting for transfers between devices, padded_2(): lax.ppermute(tail, axis, [(i, (i + 1) % count) for i in range(ends)])  9.35 us
    all_to_all x1, starting transfers between devices, local(): lax.all_to_all(jnp.stack(jnp.split(slots, lax.axis_size('gx'), axis=1)),...  5.2 us
    scatter-add x1, other arithmetic, local(): jnp.zeros((2, cells), jnp.float32).at[:, target].add(values)  5.13 us
  transfers between devices with their start and end apart: 9, of which 4 were waited for; matrix products, arithmetic and copies ran while one was open for 30% of the time, Pallas kernels for 0%

profile of v1, /device:TPU:18, one launch (start us, length us, event | category | flops | bytes accessed | tf_op | source)
XLA Modules:
  0.0 72.4 jit_solution(6660000155977564365)
XLA Ops:
  0.6 0.7 compare_select_fusion.1
  1.4 0.7 compare_and_fusion
  2.0 0.7 %fusion.156 = s32[128,4]{1,0:T(8,128)S(1)} fusion(s32[128]{0:T(128)} %bitcast.88), kind=kLoop, calls=%fused_computation.286 | loop fusion | flops 1024 | bytes 2560 | tf_op jit(solution)/shard_map/convert_element_type | solution.py:129
  2.8 0.2 reduce_window_sum.11
  2.9 0.8 %select_reduce_fusion = s32[128]{0:T(128)S(1)} fusion(s32[128,4]{1,0:T(8,128)S(1)} %reduce_window_sum.11, s32[128]{0:T(128)} %bitcast.89), kind=kLoop, calls=%fused_computation.284 | loop fusion | flops 1408 | bytes 3072 | tf_op jit(solution)/shard_map/reduce_sum | solution.py:131
  3.8 0.7 fusion.160
  4.4 0.7 convert_bitcast_fusion
  5.1 0.6 gather_fusion
  5.7 0.1 broadcast_select_fusion
  5.8 0.1 copy.31
  5.9 0.9 %scatter_custom_fusion = f32[3,256]{0,1:T(8,128)S(1)} fusion(s32[128]{0:T(128)S(1)} %fusion.160, f32[128,3]{1,0:T(8,128)S(1)} %copy.31, f32[]{:T(128)} %constant.26.clone.1), kind=kCustom, calls=%fused_computation.287 | custom fusion | bytes 3076 | tf_op jit(solution)/shard_map/scatter | solution.py:134
  7.1 0.5 broadcast.301
  7.7 0.7 reduce.8
  8.3 0.7 reshape.120
  9.0 5.2 %all-to-all-start = ((f32[4,1,192]{2,1,0:T(1,128)}), f32[4,1,192]{2,1,0:T(1,128)S(1)}, u32[]{:S(2)}, u32[]{:S(2)}) async-start(f32[4,1,192]{2,1,0:T(1,128)} %reshape.120), calls=%async_computation | async-start | bytes 8192 | tf_op jit(solution)/shard_map/all_to_all | solution.py:137
  14.2 0.8 %fusion.152 = (f32[2,4,16,128]{3,2,1,0:T(8,128)S(1)}, f32[2,4,16,128]{3,2,1,0:T(8,128)S(1)}) fusion(f32[1,8,16,128]{3,2,1,0:T(8,128)} %bitcast.64, f32[1,8,16,128]{3,2,1,0:T(8,128)} %bitcast.52), kind=kLoop, calls=%fused_computation.259 | loop fusion | flops 32768 | bytes 262144 | tf_op jit(solution)/shard_map/stack | solution.py:142
  15.0 2.5 %collective-permute-start = (f32[2,4,16,128]{3,2,1,0:T(8,128)S(1)}, f32[2,4,16,128]{3,2,1,0:T(8,128)S(1)}, u32[]{:S(2)}, u32[]{:S(2)}) collective-permute-start(f32[2,4,16,128]{3,2,1,0:T(8,128)S(1)} %get-tuple-element.42), channel_id=1, source_target_pairs={{4,0},{8,4},{12,8},{5,1},{9,5},{13,9},{6,2},{10,6},{14,10},{7,3},{... | collective-permute-start | bytes 196616 | tf_op jit(solution)/shard_map/ppermute | solution.py:20
  17.5 3.4 %collective-permute-start.1 = (f32[2,4,16,128]{3,2,1,0:T(8,128)S(1)}, f32[2,4,16,128]{3,2,1,0:T(8,128)S(1)}, u32[]{:S(2)}, u32[]{:S(2)}) collective-permute-start(f32[2,4,16,128]{3,2,1,0:T(8,128)S(1)} %get-tuple-element.41), channel_id=1, source_target_pairs={{0,4},{4,8},{8,12},{1,5},{5,9},{9,13},{2,6},{6,10},{10,14},{3,7},{... | collective-permute-start | bytes 196616 | tf_op jit(solution)/shard_map/ppermute | solution.py:18
  20.9 1.1 %fusion.172 = (f32[8,16,128]{2,1,0:T(8,128)S(1)}, f32[8,16,128]{2,1,0:T(8,128)S(1)}) fusion(f32[8,16,128]{2,1,0:T(8,128)} %param.21), kind=kLoop, calls=%fused_computation.313 | loop fusion | bytes 196608 | tf_op jit(solution)/shard_map/sin | solution.py:73
  22.0 1.1 %fusion.161 = (f32[8,16,128]{2,1,0:T(8,128)S(1)}, f32[8,16,128]{2,1,0:T(8,128)S(1)}, f32[8,16,128]{2,1,0:T(8,128)S(1)}, f32[8,16,128]{2,1,0:T(8,128)S(1)}, f32[8...) fusion(f32[8,16,128]{2,1,0:T(8,128)S(1)} %get-tuple-element.48, f32[8,16,128]{2,1,0:T(8,128)} %param.22, ...), kind=kLoop, calls=%fused_computation.310 | loop fusion | flops 163840 | bytes 589824 | tf_op jit(solution)/shard_map/mul | solution.py:77
  23.1 0.7 reduce.9
  23.8 0.1 reshape.121
  23.9 0.1 convert_element_type.37
  24.0 0.1 reshape.99
  24.0 0.1 copy.37
  24.2 5.1 %scatter_custom_fusion.1 = f32[2,16384]{0,1:T(8,128)} fusion(s32[256]{0:T(256)S(1)} %bitcast.90, f32[256,2]{1,0:T(8,128)S(1)} %copy.37, f32[]{:T(128)} %constant.26.clone.1), kind=kCustom, calls=%fused_computation.5 | custom fusion | flops 512 | bytes 131076 | tf_op jit(solution)/shard_map/scatter-add | solution.py:141
  29.3 12.3 %slice_reduce_fusion.1 = (f32[16384]{0:T(1024)S(1)}, f32[16384]{0:T(1024)S(1)}) fusion(f32[2,16384]{0,1:T(8,128)} %scatter_custom_fusion.1), kind=kLoop, calls=%fused_computation.4 | loop fusion | bytes 262144 | tf_op jit(solution)/shard_map/slice | solution.py:144
  41.7 1.9 %collective-permute-start.2 = (f32[2,16,4,128]{3,2,1,0:T(4,128)S(1)}, f32[2,16,4,128]{3,2,1,0:T(4,128)S(1)}, u32[]{:S(2)}, u32[]{:S(2)}) collective-permute-start(f32[2,16,4,128]{3,2,1,0:T(4,128)S(1)} %get-tuple-element.27), channel_id=1, source_target_pairs={{1,0},{2,1},{3,2},{5,4},{6,5},{7,6},{9,8},{10,9},{11,10},{13,12},{... | collective-permute-start | bytes 196616 | tf_op jit(solution)/shard_map/ppermute | solution.py:20
  43.7 2.5 %collective-permute-start.3 = (f32[2,16,4,128]{3,2,1,0:T(4,128)S(1)}, f32[2,16,4,128]{3,2,1,0:T(4,128)S(1)}, u32[]{:S(2)}, u32[]{:S(2)}) collective-permute-start(f32[2,16,4,128]{3,2,1,0:T(4,128)S(1)} %get-tuple-element.26), channel_id=1, source_target_pairs={{0,1},{1,2},{2,3},{4,5},{5,6},{6,7},{8,9},{9,10},{10,11},{12,13},{... | collective-permute-start | bytes 196616 | tf_op jit(solution)/shard_map/ppermute | solution.py:18
  46.3 3.1 %collective-permute-done.3 = f32[2,16,4,128]{3,2,1,0:T(4,128)S(1)} collective-permute-done((f32[2,16,4,128]{3,2,1,0:T(4,128)S(1)}, f32[2,16,4,128]{3,2,1,0:T(4,128)S(1)}, u32[]{:S(2)}, u32[]{:S(2)}) %collective-permute-start.3) | collective-permute-done | bytes 65568 | tf_op jit(solution)/shard_map/ppermute | solution.py:18
  49.4 0.4 select_maximum_fusion.5
  49.8 0.4 fusion.39
  50.3 0.7 fusion.18
  51.0 0.6 fusion.101
  51.8 3.1 %collective-permute-start.4 = (f32[2,4,16,128]{3,2,1,0:T(8,128)S(1)}, f32[2,4,16,128]{3,2,1,0:T(8,128)S(1)}, u32[]{:S(2)}, u32[]{:S(2)}) collective-permute-start(f32[2,4,16,128]{3,2,1,0:T(8,128)S(1)} %get-tuple-element.33), channel_id=1, source_target_pairs={{4,0},{8,4},{12,8},{5,1},{9,5},{13,9},{6,2},{10,6},{14,10},{7,3},{... | collective-permute-start | bytes 196616 | tf_op jit(solution)/shard_map/ppermute | solution.py:20
  54.9 2.7 %collective-permute-start.5 = (f32[2,4,16,128]{3,2,1,0:T(8,128)S(1)}, f32[2,4,16,128]{3,2,1,0:T(8,128)S(1)}, u32[]{:S(2)}, u32[]{:S(2)}) collective-permute-start(f32[2,4,16,128]{3,2,1,0:T(8,128)S(1)} %get-tuple-element.32), channel_id=1, source_target_pairs={{0,4},{4,8},{8,12},{1,5},{5,9},{9,13},{2,6},{6,10},{10,14},{3,7},{... | collective-permute-start | bytes 196616 | tf_op jit(solution)/shard_map/ppermute | solution.py:18
  57.6 0.3 collective-permute-done.4
  57.9 3.1 %collective-permute-done.5 = f32[2,4,16,128]{3,2,1,0:T(8,128)S(1)} collective-permute-done((f32[2,4,16,128]{3,2,1,0:T(8,128)S(1)}, f32[2,4,16,128]{3,2,1,0:T(8,128)S(1)}, u32[]{:S(2)}, u32[]{:S(2)}) %collective-permute-start.5) | collective-permute-done | bytes 65568 | tf_op jit(solution)/shard_map/ppermute | solution.py:18
  61.1 1.9 %collective-permute-start.6 = (f32[2,16,4,128]{3,2,1,0:T(4,128)S(1)}, f32[2,16,4,128]{3,2,1,0:T(4,128)S(1)}, u32[]{:S(2)}, u32[]{:S(2)}) collective-permute-start(f32[2,16,4,128]{3,2,1,0:T(4,128)S(1)} %get-tuple-element.23), channel_id=1, source_target_pairs={{1,0},{2,1},{3,2},{5,4},{6,5},{7,6},{9,8},{10,9},{11,10},{13,12},{... | collective-permute-start | bytes 196616 | tf_op jit(solution)/shard_map/ppermute | solution.py:20
  63.0 2.5 %collective-permute-start.7 = (f32[2,16,4,128]{3,2,1,0:T(4,128)S(1)}, f32[2,16,4,128]{3,2,1,0:T(4,128)S(1)}, u32[]{:S(2)}, u32[]{:S(2)}) collective-permute-start(f32[2,16,4,128]{3,2,1,0:T(4,128)S(1)} %get-tuple-element.22), channel_id=1, source_target_pairs={{0,1},{1,2},{2,3},{4,5},{5,6},{6,7},{8,9},{9,10},{10,11},{12,13},{... | collective-permute-start | bytes 196616 | tf_op jit(solution)/shard_map/ppermute | solution.py:18
  65.6 3.1 %collective-permute-done.7 = f32[2,16,4,128]{3,2,1,0:T(4,128)S(1)} collective-permute-done((f32[2,16,4,128]{3,2,1,0:T(4,128)S(1)}, f32[2,16,4,128]{3,2,1,0:T(4,128)S(1)}, u32[]{:S(2)}, u32[]{:S(2)}) %collective-permute-start.7) | collective-permute-done | bytes 65568 | tf_op jit(solution)/shard_map/ppermute | solution.py:18
  68.7 0.4 select_maximum_fusion
  69.2 0.4 fusion.32
  69.6 0.5 fusion.4
  70.2 0.2 fusion.11
  70.4 0.6 fusion.50
  71.0 0.7 fusion.155
  71.7 0.7 add_add_fusion
  (48 shorter events, 0.8 us)
Async XLA Ops:
  0.6 4.5 %copy-start = (f32[1024,128]{1,0:T(8,128)S(1)}, f32[1024,128]{1,0:T(8,128)}, u32[]{:S(2)}) copy-start(f32[1024,128]{1,0:T(8,128)} %param.24) | copy-start | bytes 1572868
  9.0 14.1 %all-to-all-start = ((f32[4,1,192]{2,1,0:T(1,128)}), f32[4,1,192]{2,1,0:T(1,128)S(1)}, u32[]{:S(2)}, u32[]{:S(2)}) async-start(f32[4,1,192]{2,1,0:T(1,128)} %reshape.120), calls=%async_computation | async-start | bytes 8192 | tf_op jit(solution)/shard_map/all_to_all | solution.py:137
  15.0 26.6 %collective-permute-start = (f32[2,4,16,128]{3,2,1,0:T(8,128)S(1)}, f32[2,4,16,128]{3,2,1,0:T(8,128)S(1)}, u32[]{:S(2)}, u32[]{:S(2)}) collective-permute-start(f32[2,4,16,128]{3,2,1,0:T(8,128)S(1)} %get-tuple-element.42), channel_id=1, source_target_pairs={{4,0},{8,4},{12,8},{5,1},{9,5},{13,9},{6,2},{10,6},{14,10},{7,3},{... | collective-permute-start | bytes 196616 | tf_op jit(solution)/shard_map/ppermute | solution.py:20
  17.5 24.1 %collective-permute-start.1 = (f32[2,4,16,128]{3,2,1,0:T(8,128)S(1)}, f32[2,4,16,128]{3,2,1,0:T(8,128)S(1)}, u32[]{:S(2)}, u32[]{:S(2)}) collective-permute-start(f32[2,4,16,128]{3,2,1,0:T(8,128)S(1)} %get-tuple-element.41), channel_id=1, source_target_pairs={{0,4},{4,8},{8,12},{1,5},{5,9},{9,13},{2,6},{6,10},{10,14},{3,7},{... | collective-permute-start | bytes 196616 | tf_op jit(solution)/shard_map/ppermute | solution.py:18
  29.3 12.3 %copy-start.1 = (f32[8,16,128]{2,1,0:T(8,128)S(1)}, f32[8,16,128]{2,1,0:T(8,128)}, u32[]{:S(2)}) copy-start(f32[8,16,128]{2,1,0:T(8,128)} %param.15) | copy-start | bytes 196612
  29.3 12.3 %copy-start.3 = (f32[8,16,128]{2,1,0:T(8,128)S(1)}, f32[8,16,128]{2,1,0:T(8,128)}, u32[]{:S(2)}) copy-start(f32[8,16,128]{2,1,0:T(8,128)} %param.14) | copy-start | bytes 196612
  41.7 4.6 %collective-permute-start.2 = (f32[2,16,4,128]{3,2,1,0:T(4,128)S(1)}, f32[2,16,4,128]{3,2,1,0:T(4,128)S(1)}, u32[]{:S(2)}, u32[]{:S(2)}) collective-permute-start(f32[2,16,4,128]{3,2,1,0:T(4,128)S(1)} %get-tuple-element.27), channel_id=1, source_target_pairs={{1,0},{2,1},{3,2},{5,4},{6,5},{7,6},{9,8},{10,9},{11,10},{13,12},{... | collective-permute-start | bytes 196616 | tf_op jit(solution)/shard_map/ppermute | solution.py:20
  43.6 7.9 %copy-start.5 = (f32[8,16,128]{2,1,0:T(8,128)S(1)}, f32[8,16,128]{2,1,0:T(8,128)}, u32[]{:S(2)}) copy-start(f32[8,16,128]{2,1,0:T(8,128)} %param.18) | copy-start | bytes 196612
  43.6 7.9 %copy-start.6 = (f32[8,16,128]{2,1,0:T(8,128)S(1)}, f32[8,16,128]{2,1,0:T(8,128)}, u32[]{:S(2)}) copy-start(f32[8,16,128]{2,1,0:T(8,128)} %param.20) | copy-start | bytes 196612
  43.7 7.9 %copy-start.8 = (f32[8,16,128]{2,1,0:T(8,128)S(1)}, f32[8,16,128]{2,1,0:T(8,128)}, u32[]{:S(2)}) copy-start(f32[8,16,128]{2,1,0:T(8,128)} %param.17) | copy-start | bytes 196612
  43.7 5.7 %collective-permute-start.3 = (f32[2,16,4,128]{3,2,1,0:T(4,128)S(1)}, f32[2,16,4,128]{3,2,1,0:T(4,128)S(1)}, u32[]{:S(2)}, u32[]{:S(2)}) collective-permute-start(f32[2,16,4,128]{3,2,1,0:T(4,128)S(1)} %get-tuple-element.26), channel_id=1, source_target_pairs={{0,1},{1,2},{2,3},{4,5},{5,6},{6,7},{8,9},{9,10},{10,11},{12,13},{... | collective-permute-start | bytes 196616 | tf_op jit(solution)/shard_map/ppermute | solution.py:18
  46.3 5.4 %copy-start.7 = (f32[8,16,128]{2,1,0:T(8,128)S(1)}, f32[8,16,128]{2,1,0:T(8,128)}, u32[]{:S(2)}) copy-start(f32[8,16,128]{2,1,0:T(8,128)} %param.19) | copy-start | bytes 196612
  46.3 5.4 %copy-start.9 = (f32[8,16,128]{2,1,0:T(8,128)S(1)}, f32[8,16,128]{2,1,0:T(8,128)}, u32[]{:S(2)}) copy-start(f32[8,16,128]{2,1,0:T(8,128)} %param.16) | copy-start | bytes 196612
  51.7 20.1 %copy-start.2 = (f32[8,16,128]{2,1,0:T(8,128)}, f32[8,16,128]{2,1,0:T(8,128)S(1)}, u32[]{:S(2)}) copy-start(f32[8,16,128]{2,1,0:T(8,128)S(1)} %get-tuple-element.14) | copy-start | bytes 196612
  51.8 19.2 %copy-start.4 = (f32[8,16,128]{2,1,0:T(8,128)}, f32[8,16,128]{2,1,0:T(8,128)S(1)}, u32[]{:S(2)}) copy-start(f32[8,16,128]{2,1,0:T(8,128)S(1)} %add_add_fusion.3) | copy-start | bytes 196612
  51.8 6.2 %collective-permute-start.4 = (f32[2,4,16,128]{3,2,1,0:T(8,128)S(1)}, f32[2,4,16,128]{3,2,1,0:T(8,128)S(1)}, u32[]{:S(2)}, u32[]{:S(2)}) collective-permute-start(f32[2,4,16,128]{3,2,1,0:T(8,128)S(1)} %get-tuple-element.33), channel_id=1, source_target_pairs={{4,0},{8,4},{12,8},{5,1},{9,5},{13,9},{6,2},{10,6},{14,10},{7,3},{... | collective-permute-start | bytes 196616 | tf_op jit(solution)/shard_map/ppermute | solution.py:20
  54.9 6.2 %collective-permute-start.5 = (f32[2,4,16,128]{3,2,1,0:T(8,128)S(1)}, f32[2,4,16,128]{3,2,1,0:T(8,128)S(1)}, u32[]{:S(2)}, u32[]{:S(2)}) collective-permute-start(f32[2,4,16,128]{3,2,1,0:T(8,128)S(1)} %get-tuple-element.32), channel_id=1, source_target_pairs={{0,4},{4,8},{8,12},{1,5},{5,9},{9,13},{2,6},{6,10},{10,14},{3,7},{... | collective-permute-start | bytes 196616 | tf_op jit(solution)/shard_map/ppermute | solution.py:18
  61.1 4.5 %collective-permute-start.6 = (f32[2,16,4,128]{3,2,1,0:T(4,128)S(1)}, f32[2,16,4,128]{3,2,1,0:T(4,128)S(1)}, u32[]{:S(2)}, u32[]{:S(2)}) collective-permute-start(f32[2,16,4,128]{3,2,1,0:T(4,128)S(1)} %get-tuple-element.23), channel_id=1, source_target_pairs={{1,0},{2,1},{3,2},{5,4},{6,5},{7,6},{9,8},{10,9},{11,10},{13,12},{... | collective-permute-start | bytes 196616 | tf_op jit(solution)/shard_map/ppermute | solution.py:20
  63.0 8.0 %copy-start.10 = (bf16[2,8,16,128]{3,2,1,0:T(8,128)(2,1)S(1)}, bf16[2,8,16,128]{3,2,1,0:T(8,128)(2,1)}, u32[]{:S(2)}) copy-start(bf16[2,8,16,128]{3,2,1,0:T(8,128)(2,1)} %param.23) | copy-start | bytes 196612
  63.0 5.7 %collective-permute-start.7 = (f32[2,16,4,128]{3,2,1,0:T(4,128)S(1)}, f32[2,16,4,128]{3,2,1,0:T(4,128)S(1)}, u32[]{:S(2)}, u32[]{:S(2)}) collective-permute-start(f32[2,16,4,128]{3,2,1,0:T(4,128)S(1)} %get-tuple-element.22), channel_id=1, source_target_pairs={{0,1},{1,2},{2,3},{4,5},{5,6},{6,7},{8,9},{9,10},{10,11},{12,13},{... | collective-permute-start | bytes 196616 | tf_op jit(solution)/shard_map/ppermute | solution.py:18
